TPU v7x, 32 devices: a whole 2x2x4 slice. The times are simulated.
32 devices in a mesh: dp: 4 (over x, core), seq: 8 (over z, y).
Axes of the slice: x: 2, y: 2, z: 4, core: 2. Of those that a mesh axis runs over, the one named last changes fastest.
Arguments:
- queries: bfloat16 [4, 4096, 2048], P('dp', 'seq'), may hold values from -34 to 34
- neighbour_input: bfloat16 [4, 32, 64, 896], P('dp', 'seq'), may hold values from -6 to 6
- owner_list: int32 [4, 64, 2], P('dp', 'seq'), may hold values from 0 to 7, as said below
- block_list: int32 [4, 64, 2], P('dp', 'seq'), may hold values from 0 to 3
- enc_gain: float32 [896], replicated, may hold values from 0.5 to 8
- enc_attn: bfloat16 [4, 896, 896], P(None, 'dp'), may hold values from -0.1875 to 0.1875
- kv_weight: bfloat16 [2, 896, 2048], replicated, may hold values from -0.1875 to 0.1875
Outputs:
- context: bfloat16 [4, 4096, 2048], P('dp', 'seq')
Inputs may be any that keep to these rules, and one draw needn't show every extreme that they name: `owner_list`: within the spans of one device, no owner is named more than 2 times; every owner is named in every sequence.
All inputs are finite; a program needn't handle non-finite values.
Results may differ from a plain program's by a relative error of at most 0.025.
The roundings to bfloat16 on the way count: a program that leaves them out, or rounds other values in their place, can miss the bound.
Values may be sent and summed in bfloat16 or wider, within the bound.
No kernel may reach another device: no remote copies, remote signals or barrier semaphores. Data moves between devices by JAX's collectives and lax.ppermute only.
A program may use at most 128 MiB of HBM per device.

v0:
```python
import jax
import jax.numpy as jnp
from jax import lax
from jax.sharding import PartitionSpec as P

HEADS = 16
HEAD_DIM = 128
ENC_HEADS = 7
NLEN = 64
SPAN = 64
NEIGH = 2
NB_DEV = 4
epsilon = 1e-05


def softmax_rows(scores):
    highest = jnp.max(scores, axis=-1, keepdims=True)
    raised = jnp.exp(scores - highest)
    return raised / jnp.sum(raised, axis=-1, keepdims=True)


def encode(blocks, gain, attention):
    inputs = blocks.astype(jnp.float32)
    spread = jnp.mean(inputs * inputs, axis=-1, keepdims=True)
    normed = (inputs * lax.rsqrt(spread + epsilon) * gain).astype(jnp.bfloat16)
    count, length, width = blocks.shape
    head_size = width // ENC_HEADS
    projected = jnp.einsum(
        "nte,pef->pntf", normed, attention[:3], preferred_element_type=jnp.float32
    ).astype(jnp.bfloat16)
    split_heads = projected.reshape(3, count, length, ENC_HEADS, head_size)
    scores = jnp.einsum(
        "nqhd,nkhd->nhqk", split_heads[0], split_heads[1], preferred_element_type=jnp.float32
    ) * head_size ** (-0.5)
    weights = softmax_rows(scores).astype(jnp.bfloat16)
    mixture = jnp.einsum(
        "nhqk,nkhd->nqhd", weights, split_heads[2], preferred_element_type=jnp.float32
    ).astype(jnp.bfloat16)
    mixture = mixture.reshape(count, length, width)
    output = jnp.einsum("nte,ef->ntf", mixture, attention[3], preferred_element_type=jnp.float32)
    return (inputs + output).astype(jnp.bfloat16)


def shards(queries, neighbour_input, owner_list, block_list, enc_gain, enc_attn, kv_weight):
    full_weights = lax.all_gather(enc_attn, "dp", axis=1, tiled=True)
    encoded = encode(neighbour_input[0], enc_gain, full_weights)
    owners = owner_list.reshape(-1)
    indices = block_list.reshape(-1)
    global_ids = owners * NB_DEV + indices
    piece = lax.all_gather(encoded, "seq", axis=0, tiled=True)
    selector = (global_ids[:, None] == jnp.arange(piece.shape[0], dtype=jnp.int32)[None, :]).astype(
        jnp.bfloat16
    )
    chosen = jnp.einsum("rb,bte->rte", selector, piece, preferred_element_type=jnp.float32).astype(
        jnp.bfloat16
    )
    key_value = jnp.einsum(
        "rte,pef->prtf", chosen, kv_weight, preferred_element_type=jnp.float32
    ).astype(jnp.bfloat16)
    span_count = queries.shape[1] // SPAN
    memory_keys = key_value[0].reshape(span_count, NEIGH * NLEN, HEADS, HEAD_DIM)
    memory_values = key_value[1].reshape(span_count, NEIGH * NLEN, HEADS, HEAD_DIM)
    grouped = queries[0].reshape(span_count, SPAN, HEADS, HEAD_DIM)
    scores = jnp.einsum(
        "cqhd,ckhd->chqk", grouped, memory_keys, preferred_element_type=jnp.float32
    ) * HEAD_DIM ** (-0.5)
    weights = softmax_rows(scores).astype(jnp.bfloat16)
    mixture = jnp.einsum(
        "chqk,ckhd->cqhd", weights, memory_values, preferred_element_type=jnp.float32
    ).astype(jnp.bfloat16)
    return mixture.reshape(queries.shape)


def solution(mesh):
    return jax.shard_map(
        shards,
        mesh=mesh,
        in_specs=(
            P("dp", "seq", None),
            P("dp", "seq", None, None),
            P("dp", "seq", None),
            P("dp", "seq", None),
            P(),
            P(None, "dp", None),
            P(),
        ),
        out_specs=P("dp", "seq", None),
        check_vma=False,
    )
```

profile of v0, /device:TPU:0, one launch (start us, length us, event | category | flops | bytes accessed | tf_op | source)
XLA Modules:
  0.0 194.3 jit_solution(1259733458802943780)
XLA Ops:
  6.5 0.0 all-gather.3.cloned.1.call-start
  6.5 0.7 all-gather.3.cloned.1.call-update
  7.3 0.0 all-gather.5.cloned.1.call-start
  7.3 1.2 fusion.33
  8.5 50.3 %all-gather.3.cloned.1.call-done = bf16[4,896,896]{2,1,0:T(8,128)(2,1)} async-done(((bf16[4,224,896]{2,1,0:T(8,128)(2,1)}), bf16[4,896,896]{2,1,0:T(8,128)(2,1)}) %all-gather.3.cloned.1.call-update) | async-done | bytes 6422544 | tf_op jit(solution)/shard_map/all_gather | solution.py:45
  58.8 4.3 %fusion.28 = bf16[3,4,64,896]{3,2,0,1:T(8,128)(2,1)S(1)} fusion(bf16[4,896,896]{2,1,0:T(8,128)(2,1)} %all-gather.3.cloned.1.call-done, bf16[1,4,64,896]{3,2,1,0:T(8,128)(2,1)} %param.8, f32[896]{0:T(1024)} %param.11, f32[4,64]{1,0:T(4,128)S(1)} %add_rsqrt_fusion), kind=kOutput, calls=%fused_computation.28 | convolution fusion | flops 1234731008 | bytes 6657024 | tf_op jit(solution)/shard_map/nte,pef->pntf/dot_general | solution.py:28
  63.0 0.1 fusion.65
  63.2 0.5 squeeze.14
  63.7 0.5 squeeze.15
  64.2 0.4 convolution_multiply_fusion
  64.6 0.0 copy-start.1
  64.6 0.5 fusion.66
  65.1 0.5 squeeze.13
  65.6 0.0 copy-start.2
  65.6 0.0 copy-start.3
  65.6 0.4 fusion.32
  66.1 0.0 copy-done.1
  66.1 2.9 %fusion.31 = bf16[4,64,896]{2,1,0:T(8,128)(2,1)} fusion(bf16[4,896,896]{2,1,0:T(8,128)(2,1)} %all-gather.3.cloned.1.call-done, bf16[4,7,8,8,128]{4,3,2,1,0:T(8,128)(2,1)S(1)} %fusion.32, bf16[1,4,64,896]{3,2,1,0:T(8,128)(2,1)S(1)} %copy-done.1), kind=kOutput, calls=%fused_computation.36 | convolution fusion | flops 411729920 | bytes 2981888 | tf_op jit(solution)/shard_map/nte,ef->ntf/dot_general | solution.py:40
  69.0 0.0 all-gather.5.cloned.1.call-update
  69.0 0.0 copy-done.2
  69.0 0.0 copy-done.3
  69.0 0.1 copy.26
  69.1 0.1 add.25
  69.2 2.2 %copy.45 = bf16[64,8,16,128]{3,2,1,0:T(8,128)(2,1)S(1)} copy(bf16[64,8,16,128]{3,1,2,0:T(8,128)(2,1)} %bitcast.105) | data formatting | bytes 4194304
  71.4 64.6 %all-gather.5.cloned.1.call-done = bf16[32,64,896]{2,1,0:T(8,128)(2,1)} async-done(((bf16[4,64,896]{2,1,0:T(8,128)(2,1)}), bf16[32,64,896]{2,1,0:T(8,128)(2,1)}) %all-gather.5.cloned.1.call-update) | async-done | bytes 3670032 | tf_op jit(solution)/shard_map/all_gather | solution.py:50
  136.0 5.0 %convert_bitcast_fusion.2 = bf16[16,64,896,1]{2,0,1,3:T(8,128)(2,1)S(1)} fusion(bf16[32,64,896]{2,1,0:T(8,128)(2,1)} %all-gather.5.cloned.1.call-done, s32[16]{0:T(128)S(1)} %add.25), kind=kOutput, calls=%fused_computation.24 | convolution fusion | flops 59638272 | bytes 5505088 | tf_op jit(solution)/shard_map/rb,bte->rte/dot_general | solution.py:54
  141.0 11.3 %convert_bitcast_fusion = bf16[2,16,64,2048]{3,2,0,1:T(8,128)(2,1)S(1)} fusion(bf16[2,896,2048]{2,1,0:T(8,128)(2,1)} %param.13, bf16[16,64,896,1]{2,0,1,3:T(8,128)(2,1)S(1)} %convert_bitcast_fusion.2), kind=kOutput, calls=%fused_computation.2 | convolution fusion | flops 7520387072 | bytes 17563648 | tf_op jit(solution)/shard_map/rte,pef->prtf/dot_general | solution.py:57
  152.3 1.2 fusion.64
  153.5 1.4 copy.44
  154.9 3.0 %fusion.11 = f32[8,16,128,64]{2,3,1,0:T(8,128)S(1)} fusion(bf16[8,128,16,128]{3,2,1,0:T(8,128)(2,1)S(1)} %bitcast.100, bf16[8,64,16,128]{3,2,1,0:T(8,128)(2,1)S(1)} %bitcast.103), kind=kOutput, calls=%fused_computation.13 | convolution fusion | flops 268435456 | bytes 10485760 | tf_op jit(solution)/shard_map/cqhd,ckhd->chqk/dot_general | solution.py:64
  157.9 0.0 copy-start
  157.9 2.2 %fusion.71 = f32[8,16,64]{2,1,0:T(8,128)S(1)} fusion(f32[8,16,128,64]{2,3,1,0:T(8,128)S(1)} %fusion.11), kind=kOutput, calls=%fused_computation.65 | output fusion | flops 4194431 | bytes 4227072 | tf_op jit(solution)/shard_map/sub | solution.py:18
  160.1 3.3 %copy.46 = bf16[128,8,16,128]{3,2,1,0:T(8,128)(2,1)} copy(bf16[128,8,16,128]{3,1,2,0:T(8,128)(2,1)S(1)} %bitcast.101) | data formatting | bytes 8388608
  163.4 0.0 copy-done
  163.4 18.7 %convert_bitcast_fusion.1 = bf16[8,64,16,128]{3,1,2,0:T(8,128)(2,1)} fusion(bf16[8,128,16,128]{3,2,1,0:T(8,128)(2,1)} %bitcast.104, f32[8,16,64]{2,1,0:T(8,128)S(1)} %fusion.71, f32[8,16,128,64]{2,3,1,0:T(8,128)} %copy-done), kind=kOutput, calls=%fused_computation.20 | convolution fusion | flops 274735232 | bytes 10518528 | tf_op jit(solution)/shard_map/chqk,ckhd->cqhd/dot_general | solution.py:68
  182.2 3.0 %copy.37 = bf16[8,64,16,128]{3,2,1,0:T(8,128)(2,1)S(1)} copy(bf16[8,64,16,128]{3,1,2,0:T(8,128)(2,1)} %convert_bitcast_fusion.1) | data formatting | bytes 4194304 | tf_op jit(solution)/shard_map/convert_element_type | solution.py:70
  185.1 2.3 %reshape.44 = bf16[1,512,2048]{2,1,0:T(8,128)(2,1)} reshape(bf16[8,64,16,128]{3,2,1,0:T(8,128)(2,1)S(1)} %copy.37) | data formatting | bytes 4194304 | tf_op jit(solution)/shard_map/reshape | solution.py:71
  (2 shorter events, 0.0 us)
Async XLA Ops:
  6.5 52.2 %all-gather.3.cloned.1.call-start = ((), (), s32[]{:S(2)}) async-start(), calls=%async_computation | async-start | bytes 8028160 | tf_op jit(solution)/shard_map/all_gather | solution.py:45
  7.3 128.7 %all-gather.5.cloned.1.call-start = ((), (), s32[]{:S(2)}) async-start(), calls=%async_computation.1 | async-start | bytes 4128768 | tf_op jit(solution)/shard_map/all_gather | solution.py:50
  64.6 1.5 copy-start.1
  65.6 3.4 %copy-start.2 = (s32[1,8,2]{1,2,0:T(2,128)S(1)}, s32[1,8,2]{1,2,0:T(2,128)}, u32[]{:S(2)}) copy-start(s32[1,8,2]{1,2,0:T(2,128)} %param.10) | copy-start | bytes 196
  65.6 3.4 %copy-start.3 = (s32[1,8,2]{1,2,0:T(2,128)S(1)}, s32[1,8,2]{1,2,0:T(2,128)}, u32[]{:S(2)}) copy-start(s32[1,8,2]{1,2,0:T(2,128)} %param.9) | copy-start | bytes 196
  157.9 5.6 %copy-start = (f32[8,16,128,64]{2,3,1,0:T(8,128)}, f32[8,16,128,64]{2,3,1,0:T(8,128)S(1)}, u32[]{:S(2)}) copy-start(f32[8,16,128,64]{2,3,1,0:T(8,128)S(1)} %fusion.11) | copy-start | bytes 12582916
Sparse Core Ops, SparseCore 0:
  8.9 49.8 all-gather.2
  69.1 66.8 all-gather.4
where the time goes:
time: 195 us; the launch traced here: 194 us
  waiting for transfers between devices  116 us (59%)
  matrix products  46.4 us (24%)
  local copies, waits for them, and re-layouts  15.3 us (8%)
  between operations  13.5 us (7%)
  other arithmetic  3.45 us (2%)
    all_gather x1, waiting for transfers between devices, shards(): piece = lax.all_gather(encoded, 'seq', axis=0, tiled=True)  64.6 us
    all_gather x1, waiting for transfers between devices, shards(): full_weights = lax.all_gather(enc_attn, 'dp', axis=1, tiled=True)  50.3 us
    dot_general x1, matrix products, shards(): jnp.einsum('chqk,ckhd->cqhd', weights, memory_values, preferred_element_t...  18.7 us
    dot_general x1, matrix products, shards(): jnp.einsum('rte,pef->prtf', chosen, kv_weight, preferred_element_type=jnp...  11.3 us
    unnamed x11, local copies, waits for them, and re-layouts  6.96 us
    dot_general x1, matrix products, shards(): jnp.einsum('rb,bte->rte', selector, piece, preferred_element_type=jnp.flo...  5.01 us
    dot_general x1, matrix products, encode(): jnp.einsum('nte,pef->pntf', normed, attention[:3], preferred_element_type...  4.25 us
  transfers between devices with their start and end apart: 2, of which 2 were waited for; matrix products, arithmetic and copies ran while one was open for 2% of the time, Pallas kernels for 0%

commit v1 on v0

--- a/solution.py
+++ b/solution.py
@@ -47,7 +47,12 @@
     owners = owner_list.reshape(-1)
     indices = block_list.reshape(-1)
     global_ids = owners * NB_DEV + indices
-    piece = lax.all_gather(encoded, "seq", axis=0, tiled=True)
+    ring = [encoded]
+    for hop in range(7):
+        ring.append(lax.ppermute(ring[-1], "seq", [(dev, (dev + 1) % 8) for dev in range(8)]))
+    piece = jnp.roll(
+        jnp.concatenate(ring[::-1], axis=0), (lax.axis_index("seq") + 1) * ring[0].shape[0], axis=0
+    )
     selector = (global_ids[:, None] == jnp.arange(piece.shape[0], dtype=jnp.int32)[None, :]).astype(
         jnp.bfloat16
     )

time: 195 us -> 225 us (1.15)
  waiting for transfers between devices: 116 us -> 138 us
  local copies, waits for them, and re-layouts: 15.3 us -> 26 us
  matrix products: 46.4 us -> 41.9 us
    ppermute x0 -> x7, waiting for transfers between devices: none -> 87 us  [shards(): lax.ppermute(ring[-1], 'seq', [(dev, (dev + 1) % 8) for dev in range(8)])]
    all_gather x1 -> x0, waiting for transfers between devices: 64.6 us -> none  [shards(): piece = lax.all_gather(encoded, 'seq', axis=0, tiled=True)]
    unnamed x11 -> x42, local copies, waits for them, and re-layouts: 6.96 us -> 17.3 us
  transfers between devices with their start and end apart: 2 -> 8, of which waited for: 2 -> 8; matrix products, arithmetic and copies ran while one was open for 2% -> 2% of each run, Pallas kernels for 0% -> 0%
where the time goes in v1:
time: 225 us
  waiting for transfers between devices  138 us (61%)
  matrix products  41.9 us (19%)
  local copies, waits for them, and re-layouts  26 us (12%)
  between operations  13.7 us (6%)
  other arithmetic  3.45 us (2%)
    ppermute x7, waiting for transfers between devices, shards(): lax.ppermute(ring[-1], 'seq', [(dev, (dev + 1) % 8) for dev in range(8)])  87 us
    all_gather x1, waiting for transfers between devices, shards(): full_weights = lax.all_gather(enc_attn, 'dp', axis=1, tiled=True)  50.3 us
    dot_general x1, matrix products, shards(): jnp.einsum('chqk,ckhd->cqhd', weights, memory_values, preferred_element_t...  18.6 us
    unnamed x42, local copies, waits for them, and re-layouts  17.3 us
    dot_general x1, matrix products, shards(): jnp.einsum('rte,pef->prtf', chosen, kv_weight, preferred_element_type=jnp...  9.67 us
  transfers between devices with their start and end apart: 8, of which 8 were waited for; matrix products, arithmetic and copies ran while one was open for 2% of the time, Pallas kernels for 0%

profile of v1, /device:TPU:0, one launch (start us, length us, event | category | flops | bytes accessed | tf_op | source)
XLA Modules:
  0.0 224.7 jit_solution(9346381169135983148)
XLA Ops:
  6.5 0.7 all-gather.2.cloned.1.call-update
  7.3 1.2 fusion.32
  8.5 50.3 %all-gather.2.cloned.1.call-done = bf16[4,896,896]{2,1,0:T(8,128)(2,1)} async-done(((bf16[4,224,896]{2,1,0:T(8,128)(2,1)}), bf16[4,896,896]{2,1,0:T(8,128)(2,1)}) %all-gather.2.cloned.1.call-update) | async-done | bytes 6422544 | tf_op jit(solution)/shard_map/all_gather | solution.py:45
  58.8 4.3 %fusion.27 = bf16[3,4,64,896]{3,2,0,1:T(8,128)(2,1)S(1)} fusion(bf16[4,896,896]{2,1,0:T(8,128)(2,1)} %all-gather.2.cloned.1.call-done, bf16[1,4,64,896]{3,2,1,0:T(8,128)(2,1)} %param.8, f32[896]{0:T(1024)} %param.11, f32[4,64]{1,0:T(4,128)S(1)} %add_rsqrt_fusion), kind=kOutput, calls=%fused_computation.28 | convolution fusion | flops 1234731008 | bytes 6657024 | tf_op jit(solution)/shard_map/nte,pef->pntf/dot_general | solution.py:28
  63.0 0.1 fusion.64
  63.2 0.5 squeeze.14
  63.7 0.5 squeeze.15
  64.2 0.4 convolution_multiply_fusion
  64.6 0.5 fusion.65
  65.1 0.5 squeeze.13
  65.6 0.4 fusion.31
  66.1 2.1 fusion.30
  68.2 1.5 collective-permute-start
  69.7 13.9 %collective-permute-done = bf16[4,64,896]{2,1,0:T(8,128)(2,1)S(1)} collective-permute-done((bf16[4,64,896]{2,1,0:T(8,128)(2,1)S(1)}, bf16[4,64,896]{2,1,0:T(8,128)(2,1)S(1)}, u32[]{:S(2)}, u32[]{:S(2)}) %collective-permute-start) | collective-permute-done | bytes 458784 | tf_op jit(solution)/shard_map/ppermute | solution.py:52
  83.6 14.6 %collective-permute-done.1 = bf16[4,64,896]{2,1,0:T(8,128)(2,1)S(1)} collective-permute-done((bf16[4,64,896]{2,1,0:T(8,128)(2,1)S(1)}, bf16[4,64,896]{2,1,0:T(8,128)(2,1)S(1)}, u32[]{:S(2)}, u32[]{:S(2)}) %collective-permute-start.1) | collective-permute-done | bytes 458784 | tf_op jit(solution)/shard_map/ppermute | solution.py:52
  98.2 13.6 %collective-permute-done.2 = bf16[4,64,896]{2,1,0:T(8,128)(2,1)S(1)} collective-permute-done((bf16[4,64,896]{2,1,0:T(8,128)(2,1)S(1)}, bf16[4,64,896]{2,1,0:T(8,128)(2,1)S(1)}, u32[]{:S(2)}, u32[]{:S(2)}) %collective-permute-start.2) | collective-permute-done | bytes 458784 | tf_op jit(solution)/shard_map/ppermute | solution.py:52
  111.9 0.8 copy-done.1
  112.6 12.7 %collective-permute-done.3 = bf16[4,64,896]{2,1,0:T(8,128)(2,1)S(1)} collective-permute-done((bf16[4,64,896]{2,1,0:T(8,128)(2,1)S(1)}, bf16[4,64,896]{2,1,0:T(8,128)(2,1)S(1)}, u32[]{:S(2)}, u32[]{:S(2)}) %collective-permute-start.3) | collective-permute-done | bytes 458784 | tf_op jit(solution)/shard_map/ppermute | solution.py:52
  125.4 0.8 copy-done.3
  126.1 11.8 %collective-permute-done.4 = bf16[4,64,896]{2,1,0:T(8,128)(2,1)S(1)} collective-permute-done((bf16[4,64,896]{2,1,0:T(8,128)(2,1)S(1)}, bf16[4,64,896]{2,1,0:T(8,128)(2,1)S(1)}, u32[]{:S(2)}, u32[]{:S(2)}) %collective-permute-start.4) | collective-permute-done | bytes 458784 | tf_op jit(solution)/shard_map/ppermute | solution.py:52
  137.9 0.8 copy-done.5
  138.7 11.3 %collective-permute-done.5 = bf16[4,64,896]{2,1,0:T(8,128)(2,1)} collective-permute-done((bf16[4,64,896]{2,1,0:T(8,128)(2,1)S(1)}, bf16[4,64,896]{2,1,0:T(8,128)(2,1)}, u32[]{:S(2)}, u32[]{:S(2)}) %collective-permute-start.5) | collective-permute-done | bytes 458784 | tf_op jit(solution)/shard_map/ppermute | solution.py:52
  150.0 0.1 copy.16
  150.1 0.1 add.38
  150.2 2.2 copy.33
  152.4 9.1 %collective-permute-done.6 = bf16[4,64,896]{2,1,0:T(8,128)(2,1)} collective-permute-done((bf16[4,64,896]{2,1,0:T(8,128)(2,1)}, bf16[4,64,896]{2,1,0:T(8,128)(2,1)}, u32[]{:S(2)}, u32[]{:S(2)}) %collective-permute-start.6) | collective-permute-done | bytes 458784 | tf_op jit(solution)/shard_map/ppermute | solution.py:52
  161.5 1.1 constant_dynamic-update-slice_fusion.15
  162.5 1.1 constant_dynamic-update-slice_fusion.14
  163.7 1.1 constant_dynamic-update-slice_fusion.13
  164.8 1.1 constant_dynamic-update-slice_fusion.12
  165.9 1.1 constant_dynamic-update-slice_fusion.11
  167.0 0.1 constant_dynamic-update-slice_fusion.10
  167.2 1.1 constant_dynamic-update-slice_fusion.7
  168.3 1.1 constant_dynamic-update-slice_fusion.6
  169.4 0.1 constant_dynamic-update-slice_fusion.5
  169.4 0.1 constant_dynamic-update-slice_fusion.4
  169.5 0.1 constant_dynamic-update-slice_fusion.3
  169.8 0.3 constant_dynamic-slice_fusion
  170.1 3.0 %fusion.14 = bf16[16,64,896]{2,0,1:T(8,128)(2,1)S(1)} fusion(bf16[32,64,896]{2,1,0:T(8,128)(2,1)S(1)} %constant_dynamic-slice_fusion, s32[16]{0:T(128)S(1)} %add.38), kind=kOutput, calls=%fused_computation.18 | convolution fusion | flops 58720768 | bytes 5505088 | tf_op jit(solution)/shard_map/rb,bte->rte/dot_general | solution.py:59
  173.1 9.7 %convert_bitcast_fusion = bf16[2,16,64,2048]{3,2,0,1:T(8,128)(2,1)S(1)} fusion(bf16[2,896,2048]{2,1,0:T(8,128)(2,1)S(1)} %bitcast.110, bf16[16,64,896]{2,0,1:T(8,128)(2,1)S(1)} %fusion.14), kind=kOutput, calls=%fused_computation.2 | convolution fusion | flops 7520387072 | bytes 17563648 | tf_op jit(solution)/shard_map/rte,pef->prtf/dot_general | solution.py:62
  182.8 1.2 fusion.63
  184.0 1.4 copy.32
  185.4 3.0 %fusion.11 = f32[8,16,128,64]{2,3,1,0:T(8,128)S(1)} fusion(bf16[8,128,16,128]{3,2,1,0:T(8,128)(2,1)S(1)} %bitcast.103, bf16[8,64,16,128]{3,2,1,0:T(8,128)(2,1)S(1)} %bitcast.106), kind=kOutput, calls=%fused_computation.13 | convolution fusion | flops 268435456 | bytes 10485760 | tf_op jit(solution)/shard_map/cqhd,ckhd->chqk/dot_general | solution.py:69
  188.4 2.2 fusion.70
  190.6 3.3 %copy.34 = bf16[128,8,16,128]{3,2,1,0:T(8,128)(2,1)} copy(bf16[128,8,16,128]{3,1,2,0:T(8,128)(2,1)S(1)} %bitcast.104) | data formatting | bytes 8388608
  194.0 18.6 %convert_bitcast_fusion.1 = bf16[8,64,16,128]{3,1,2,0:T(8,128)(2,1)} fusion(bf16[8,128,16,128]{3,2,1,0:T(8,128)(2,1)} %bitcast.107, f32[8,16,64]{2,1,0:T(8,128)S(1)} %fusion.70, f32[8,16,128,64]{2,3,1,0:T(8,128)} %copy-done), kind=kOutput, calls=%fused_computation.21 | convolution fusion | flops 274735232 | bytes 10518528 | tf_op jit(solution)/shard_map/chqk,ckhd->cqhd/dot_general | solution.py:73
  212.6 3.0 %copy.25 = bf16[8,64,16,128]{3,2,1,0:T(8,128)(2,1)S(1)} copy(bf16[8,64,16,128]{3,1,2,0:T(8,128)(2,1)} %convert_bitcast_fusion.1) | data formatting | bytes 4194304 | tf_op jit(solution)/shard_map/convert_element_type | solution.py:75
  215.6 2.3 %reshape.44 = bf16[1,512,2048]{2,1,0:T(8,128)(2,1)} reshape(bf16[8,64,16,128]{3,2,1,0:T(8,128)(2,1)S(1)} %copy.25) | data formatting | bytes 4194304 | tf_op jit(solution)/shard_map/reshape | solution.py:76
  (36 shorter events, 0.3 us)
Async XLA Ops:
  6.5 52.2 %all-gather.2.cloned.1.call-start = ((), (), s32[]{:S(2)}) async-start(), calls=%async_computation | async-start | bytes 8028160 | tf_op jit(solution)/shard_map/all_gather | solution.py:45
  64.6 1.5 copy-start.7
  65.6 84.4 %copy-start.8 = (s32[1,8,2]{1,2,0:T(2,128)S(1)}, s32[1,8,2]{1,2,0:T(2,128)}, u32[]{:S(2)}) copy-start(s32[1,8,2]{1,2,0:T(2,128)} %param.10) | copy-start | bytes 196
  65.6 84.4 %copy-start.9 = (s32[1,8,2]{1,2,0:T(2,128)S(1)}, s32[1,8,2]{1,2,0:T(2,128)}, u32[]{:S(2)}) copy-start(s32[1,8,2]{1,2,0:T(2,128)} %param.9) | copy-start | bytes 196
  68.2 15.4 %collective-permute-start = (bf16[4,64,896]{2,1,0:T(8,128)(2,1)S(1)}, bf16[4,64,896]{2,1,0:T(8,128)(2,1)S(1)}, u32[]{:S(2)}, u32[]{:S(2)}) collective-permute-start(bf16[4,64,896]{2,1,0:T(8,128)(2,1)S(1)} %fusion.30), channel_id=1, source_target_pairs={{0,1},{1,2},{2,3},{3,4},{4,5},{5,6},{6,7},{7,0},{8,9},{9,10},{10,1... | collective-permute-start | bytes 1376264 | tf_op jit(solution)/shard_map/ppermute | solution.py:52
  83.6 14.6 %collective-permute-start.1 = (bf16[4,64,896]{2,1,0:T(8,128)(2,1)S(1)}, bf16[4,64,896]{2,1,0:T(8,128)(2,1)S(1)}, u32[]{:S(2)}, u32[]{:S(2)}) collective-permute-start(bf16[4,64,896]{2,1,0:T(8,128)(2,1)S(1)} %collective-permute-done), channel_id=1, source_target_pairs={{0,1},{1,2},{2,3},{3,4},{4,5},{5,6},{6,7},{7,0},{8,9},{9,10},{10,1... | collective-permute-start | bytes 1376264 | tf_op jit(solution)/shard_map/ppermute | solution.py:52
  98.2 13.7 %collective-permute-start.2 = (bf16[4,64,896]{2,1,0:T(8,128)(2,1)S(1)}, bf16[4,64,896]{2,1,0:T(8,128)(2,1)S(1)}, u32[]{:S(2)}, u32[]{:S(2)}) collective-permute-start(bf16[4,64,896]{2,1,0:T(8,128)(2,1)S(1)} %collective-permute-done.1), channel_id=1, source_target_pairs={{0,1},{1,2},{2,3},{3,4},{4,5},{5,6},{6,7},{7,0},{8,9},{9,10},{10,1... | collective-permute-start | bytes 1376264 | tf_op jit(solution)/shard_map/ppermute | solution.py:52
  111.9 0.8 copy-start.1
  112.6 12.7 %collective-permute-start.3 = (bf16[4,64,896]{2,1,0:T(8,128)(2,1)S(1)}, bf16[4,64,896]{2,1,0:T(8,128)(2,1)S(1)}, u32[]{:S(2)}, u32[]{:S(2)}) collective-permute-start(bf16[4,64,896]{2,1,0:T(8,128)(2,1)S(1)} %collective-permute-done.2), channel_id=1, source_target_pairs={{0,1},{1,2},{2,3},{3,4},{4,5},{5,6},{6,7},{7,0},{8,9},{9,10},{10,1... | collective-permute-start | bytes 1376264 | tf_op jit(solution)/shard_map/ppermute | solution.py:52
  125.4 0.8 copy-start.3
  126.1 11.8 %collective-permute-start.4 = (bf16[4,64,896]{2,1,0:T(8,128)(2,1)S(1)}, bf16[4,64,896]{2,1,0:T(8,128)(2,1)S(1)}, u32[]{:S(2)}, u32[]{:S(2)}) collective-permute-start(bf16[4,64,896]{2,1,0:T(8,128)(2,1)S(1)} %collective-permute-done.3), channel_id=1, source_target_pairs={{0,1},{1,2},{2,3},{3,4},{4,5},{5,6},{6,7},{7,0},{8,9},{9,10},{10,1... | collective-permute-start | bytes 1376264 | tf_op jit(solution)/shard_map/ppermute | solution.py:52
  137.9 0.8 copy-start.5
  138.7 11.3 %collective-permute-start.5 = (bf16[4,64,896]{2,1,0:T(8,128)(2,1)S(1)}, bf16[4,64,896]{2,1,0:T(8,128)(2,1)}, u32[]{:S(2)}, u32[]{:S(2)}) collective-permute-start(bf16[4,64,896]{2,1,0:T(8,128)(2,1)S(1)} %collective-permute-done.4), channel_id=1, source_target_pairs={{0,1},{1,2},{2,3},{3,4},{4,5},{5,6},{6,7},{7,0},{8,9},{9,10},{10,1... | collective-permute-start | bytes 1376264 | tf_op jit(solution)/shard_map/ppermute | solution.py:52
  150.0 11.5 %collective-permute-start.6 = (bf16[4,64,896]{2,1,0:T(8,128)(2,1)}, bf16[4,64,896]{2,1,0:T(8,128)(2,1)}, u32[]{:S(2)}, u32[]{:S(2)}) collective-permute-start(bf16[4,64,896]{2,1,0:T(8,128)(2,1)} %collective-permute-done.5), channel_id=1, source_target_pairs={{0,1},{1,2},{2,3},{3,4},{4,5},{5,6},{6,7},{7,0},{8,9},{9,10},{10,1... | collective-permute-start | bytes 1376264 | tf_op jit(solution)/shard_map/ppermute | solution.py:52
  162.5 6.8 %copy-start.6 = (bf16[4,64,896]{2,1,0:T(8,128)(2,1)S(1)}, bf16[4,64,896]{2,1,0:T(8,128)(2,1)}, u32[]{:S(2)}) copy-start(bf16[4,64,896]{2,1,0:T(8,128)(2,1)} %copy-done.5) | copy-start | bytes 1376260
  163.7 5.7 %copy-start.4 = (bf16[4,64,896]{2,1,0:T(8,128)(2,1)S(1)}, bf16[4,64,896]{2,1,0:T(8,128)(2,1)}, u32[]{:S(2)}) copy-start(bf16[4,64,896]{2,1,0:T(8,128)(2,1)} %copy-done.3) | copy-start | bytes 1376260
  164.8 4.7 %copy-start.2 = (bf16[4,64,896]{2,1,0:T(8,128)(2,1)S(1)}, bf16[4,64,896]{2,1,0:T(8,128)(2,1)}, u32[]{:S(2)}) copy-start(bf16[4,64,896]{2,1,0:T(8,128)(2,1)} %copy-done.1) | copy-start | bytes 1376260
  169.7 3.4 %slice-start = ((s8[7340032]{0:T(1024)(128)(4,1)}), s8[4194304]{0:T(1024)(128)(4,1)S(1)}, s32[]{:S(2)}) async-start(s8[7340032]{0:T(1024)(128)(4,1)} %bitcast.109), calls=%async_computation.1 | async-start | bytes 8388608
  169.7 3.3 %slice-start.1 = ((s8[7340032]{0:T(1024)(128)(4,1)}), s8[3145728]{0:T(1024)(128)(4,1)S(1)}, s32[]{:S(2)}) async-start(s8[7340032]{0:T(1024)(128)(4,1)} %bitcast.109), calls=%async_computation.2 | async-start | bytes 6291456
  188.4 5.6 %copy-start = (f32[8,16,128,64]{2,3,1,0:T(8,128)}, f32[8,16,128,64]{2,3,1,0:T(8,128)S(1)}, u32[]{:S(2)}) copy-start(f32[8,16,128,64]{2,3,1,0:T(8,128)S(1)} %fusion.11) | copy-start | bytes 12582916
Sparse Core Ops, SparseCore 0:
  8.9 49.8 all-gather.1
